TPU v7x, 32 devices: a whole 2x2x4 slice. The times are simulated.
32 devices in a mesh: tm: 4 (over y, x), series: 8 (over z, core).
Axes of the slice: x: 2, y: 2, z: 4, core: 2. Of those that a mesh axis runs over, the one named last changes fastest.
Arguments:
- codes: int32 [8, 512], P(None, ('tm', 'series')), may hold values from 0 to 916478, as said below
- owner_slot: int32 [8], replicated, may hold values from 0 to 7, each once
- edges: int32 [4096], replicated, may hold values from 0 to 2096640, as said below
- w_in: bfloat16 [128, 2304], replicated, may hold values from -0.09375 to 0.09375
- w_dt: bfloat16 [128, 32], replicated, may hold values from -0.5 to 0.5
- dt_bias: float32 [32], replicated, may hold values from -1 to 1
- decay_rate: float32 [32], replicated, may hold values from 1e-05 to 0.1
- grad_out: bfloat16 [8, 512, 2048], P('series', 'tm'), may hold values from -6 to 6
Outputs:
- ssd_output: bfloat16 [8, 512, 2048], P('series', 'tm')
- grad_in: float32 [128, 2304], replicated
Inputs may be any that keep to these rules, and one draw needn't show every extreme that they name: `codes`: each row is one series in the order of ingestion slots. edges[0] is 0 and edges rise strictly.
All inputs are finite; a program needn't handle non-finite values.
Results may differ from a plain program's by a relative error of at most 0.0062.
The roundings to bfloat16 on the way count: a program that leaves them out, or rounds other values in their place, can miss the bound.
Values sent between devices are 32-bit elements; how exact they have to be, the bound alone decides.
No kernel may reach another device: no remote copies, remote signals or barrier semaphores. Data moves between devices by JAX's collectives and lax.ppermute only.
A program may use at most 128 MiB of HBM per device.

v0:
```python
import math
import jax
import jax.numpy as jnp
from jax import lax
from jax.sharding import PartitionSpec as P

code_ceiling = 2097152.0


def decay_matrix(cum_decay):
    row_count = cum_decay.shape[0]
    causal = jnp.arange(row_count)[:, None] >= jnp.arange(row_count)[None, :]
    log_span = cum_decay.T[:, :, None] - cum_decay.T[:, None, :]
    return jnp.where(causal[None], jnp.exp(jnp.where(causal[None], log_span, -60.0)), 0.0)


def on_device(codes, owner_slot, edges, w_in, w_dt, dt_bias, decay_rate, grad_out):
    fl = jnp.float32
    half = jnp.bfloat16
    tok_rows = grad_out.shape[1]
    head_count = dt_bias.shape[0]
    inner_width = grad_out.shape[2]
    head_dim = inner_width // head_count
    state_dim = (w_in.shape[1] - inner_width) // 2
    n_blocks = lax.axis_size("tm")
    seq_len = tok_rows * n_blocks
    series_count = lax.axis_size("series")
    my_block = lax.axis_index("tm")
    my_series = lax.axis_index("series")
    all_codes = lax.all_gather(codes, ("tm", "series"), axis=1, tiled=True)
    row = lax.dynamic_index_in_dim(all_codes, owner_slot[my_series], axis=0, keepdims=False)
    reading = row.astype(fl)
    edge_float = edges.astype(fl)
    upper_edge = jnp.concatenate([edge_float[1:], jnp.full((1,), code_ceiling, fl)])
    onehot = (
        (edge_float[None, :] <= reading[:, None]) & (upper_edge[None, :] > reading[:, None])
    ).astype(fl)
    counts = jnp.sum(onehot, axis=0)
    before = jnp.cumsum(counts) - counts
    bin_table = jnp.stack([before, counts, edge_float, upper_edge - edge_float], axis=1)
    picked = jnp.dot(onehot, bin_table, precision=lax.Precision.HIGHEST)
    within_bin = (reading - picked[:, 2]) / picked[:, 3]
    quantile = (picked[:, 0] + picked[:, 1] * within_bin) / seq_len
    frequency = (jnp.arange(w_in.shape[0], dtype=fl) + 0.5) * math.pi
    features_all = jnp.cos(quantile[:, None] * frequency).astype(half)
    projected_all = jnp.dot(features_all, w_in, preferred_element_type=fl).astype(half)
    projected_all = projected_all.reshape(n_blocks, tok_rows, -1)
    x_all = projected_all[:, :, :inner_width].reshape(n_blocks, tok_rows, head_count, head_dim)
    b_all = projected_all[:, :, inner_width : inner_width + state_dim]
    c_all = projected_all[:, :, inner_width + state_dim :]
    step_all = jax.nn.softplus(
        dt_bias + jnp.dot(features_all, w_dt, preferred_element_type=fl)
    ).reshape(n_blocks, tok_rows, head_count)
    cum_all = jnp.cumsum(-step_all * decay_rate, axis=1)
    gate_all = jnp.exp(cum_all[:, -1])
    tail_all = jnp.exp(cum_all[:, -1:, :] - cum_all) * step_all
    xw_all = (x_all * tail_all[..., None]).astype(half)
    state_local_all = jnp.einsum("bthp,btn->bhpn", xw_all, b_all, preferred_element_type=fl)
    state_in = jnp.zeros((head_count, head_dim, state_dim), fl)
    for k in range(n_blocks - 1):
        new = gate_all[k][:, None, None] * state_in + state_local_all[k]
        state_in = jnp.where(k < my_block, new, state_in)

    def mine(a):
        return lax.dynamic_index_in_dim(a, my_block, axis=0, keepdims=False)

    features = mine(features_all.reshape(n_blocks, tok_rows, -1))
    x_heads = mine(x_all)
    b_proj = mine(b_all)
    c_proj = mine(c_all)
    step_size = mine(step_all)
    cum_decay = mine(cum_all)
    tail_factor = mine(tail_all)
    x_weighted = mine(xw_all)
    head_factor = jnp.exp(cum_decay)
    grad_heads = grad_out[0].reshape(tok_rows, head_count, head_dim)
    grad_weighted = (grad_heads * head_factor[:, :, None]).astype(half)
    adjoint_local = jnp.einsum("thp,tn->hpn", grad_weighted, c_proj, preferred_element_type=fl)
    adjoint_all = lax.all_gather(adjoint_local, "tm")
    adjoint_in = jnp.zeros((head_count, head_dim, state_dim), fl)
    for k in range(n_blocks - 1, 0, -1):
        new = gate_all[k][:, None, None] * adjoint_in + adjoint_all[k]
        adjoint_in = jnp.where(k > my_block, new, adjoint_in)
    masked = decay_matrix(cum_decay) * step_size.T[:, None, :]
    scores = jnp.dot(c_proj, b_proj.T, preferred_element_type=fl)
    weights = (scores[None] * masked).astype(half)
    state_half = state_in.astype(half)
    adjoint_half = adjoint_in.astype(half)
    output = jnp.einsum("hts,shp->thp", weights, x_heads, preferred_element_type=fl)
    output = (
        output
        + jnp.einsum("tn,hpn->thp", c_proj, state_half, preferred_element_type=fl)
        * head_factor[:, :, None]
    )
    ssd_output = output.reshape(1, tok_rows, inner_width).astype(half)
    grad_x = jnp.einsum("hts,thp->shp", weights, grad_heads, preferred_element_type=fl)
    grad_x = (
        grad_x
        + jnp.einsum("sn,hpn->shp", b_proj, adjoint_half, preferred_element_type=fl)
        * tail_factor[:, :, None]
    )
    pair_scores = jnp.einsum("thp,shp->hts", grad_heads, x_heads, preferred_element_type=fl)
    pair_mixed = jnp.sum(pair_scores * masked, axis=0).astype(half)
    grad_b = jnp.dot(pair_mixed.T, c_proj, preferred_element_type=fl)
    grad_b = grad_b + jnp.einsum("shp,hpn->sn", x_weighted, adjoint_half, preferred_element_type=fl)
    grad_c = jnp.dot(pair_mixed, b_proj, preferred_element_type=fl)
    grad_c = grad_c + jnp.einsum(
        "thp,hpn->tn", grad_weighted, state_half, preferred_element_type=fl
    )
    grad_rows = jnp.concatenate(
        [
            grad_x.reshape(tok_rows, inner_width).astype(half),
            grad_b.astype(half),
            grad_c.astype(half),
        ],
        axis=1,
    )
    local_grad = jnp.einsum("tf,tw->fw", features, grad_rows, preferred_element_type=fl)
    share_grad = lax.psum_scatter(local_grad, "series", scatter_dimension=1, tiled=True)
    share_grad = lax.psum(share_grad, "tm")
    total_grad = lax.all_gather(share_grad, "series", axis=1, tiled=True)
    grad_in = total_grad / math.sqrt(series_count * seq_len)
    return (ssd_output, grad_in)


def solution(mesh):
    return jax.shard_map(
        on_device,
        mesh=mesh,
        in_specs=(P(None, ("tm", "series")), P(), P(), P(), P(), P(), P(), P("series", "tm", None)),
        out_specs=(P("series", "tm", None), P()),
        check_vma=False,
    )
```

profile of v0, /device:TPU:0, one launch (start us, length us, event | category | flops | bytes accessed | tf_op | source)
XLA Modules:
  0.0 243.4 jit_solution(498775291195324287)
XLA Ops:
  7.2 1.3 dynamic_slice.34
  9.8 44.0 %all-gather.1 = s32[32,16,8]{1,2,0:T(8,128)S(1)} all-gather(s32[1,16,8]{1,2,0:T(8,128)} %bitcast.172), channel_id=1, replica_groups=mesh['tm'=4,'series'=8] {'tm','series'}, dimensions={0}, use_global_device_ids=true | all-gather | bytes 16896 | tf_op jit(solution)/shard_map/all_gather | solution.py:30
  56.2 1.4 convert_reduce_fusion
  58.3 4.1 %fusion = f32[512,4]{0,1:T(4,128)S(1)} fusion(f32[4096]{0:T(1024)S(1)} %get-tuple-element.13, f32[4096]{0:T(1024)S(1)} %convert_element_type.97, f32[512]{0:T(512)S(1)} %bitcast.168, f32[4096,1]{0,1:T(1,128)S(1)} %bitcast.166, f32[4096,1]{0,1:T(1,128)S(1)} %bitcast.155, f32[4096,1]{0,1:T(1,128)S(1)} %bitcast.154, f32[4096,1]{0,1:T(1,128)S(1)} %sub.42), kind=kOutput, calls=%fused_computation.2 | convolution fusion | flops 107003904 | bytes 108544 | tf_op jit(solution)/shard_map/dot_general | solution.py:41
  62.5 1.6 convolution_convert_fusion
  68.9 1.5 copy.57
  71.1 2.0 copy.61
  75.1 2.0 fusion.59
  77.4 1.6 slice.98
  79.6 3.2 %copy.54 = bf16[4,128,2048]{1,2,0:T(8,128)(2,1)S(1)} copy(bf16[4,128,2048]{2,1,0:T(8,128)(2,1)} %slice.98) | data formatting | bytes 4194304 | tf_op jit(solution)/shard_map/slice | solution.py:48
  84.0 1.7 exponential_multiply_fusion
  90.4 1.4 multiply_bitcast_fusion
  91.9 2.4 fusion.4
  96.3 2.3 convolution_bitcast_fusion
  99.3 3.6 %fusion.41 = f32[4,32,64,128]{3,2,1,0:T(8,128)} fusion(bf16[4,128,32,64]{1,3,2,0:T(8,128)(2,1)S(1)} %multiply_convert_fusion, bf16[4,128,2304]{2,1,0:T(8,128)(2,1)} %bitcast.143), kind=kOutput, calls=%fused_computation.67 | convolution fusion | flops 268435456 | bytes 6422528 | tf_op jit(solution)/shard_map/bthp,btn->bhpn/dot_general | solution.py:58
  102.9 23.4 %all-gather.7.cloned.1.call-done = f32[128,64,128]{2,1,0:T(8,128)} async-done(((f32[32,64,128]{2,1,0:T(8,128)}), f32[128,64,128]{2,1,0:T(8,128)}) %all-gather.7.cloned.1.call-update) | async-done | bytes 4194320 | tf_op jit(solution)/shard_map/all_gather | solution.py:79
  126.3 3.6 %fusion.15 = (bf16[1,32,64,128]{3,2,1,0:T(8,128)(2,1)S(1)}, bf16[1,32,64,128]{3,2,1,0:T(8,128)(2,1)S(1)}) fusion(f32[128,64,128]{2,1,0:T(8,128)} %all-gather.7.cloned.1.call-done, f32[32]{0:T(128)S(1)} %copy-done.19, f32[32]{0:T(128)S(1)} %copy-done.21, f32[32]{0:T(128)S(1)} %copy-done.22, pred[]{:T(512)S(6)} %lt.34, pred[]{:T(512)S(6)} %lt.33, pred[]{:T(512)S(6)} %lt.32, ...), kind=kLoop, calls=%fused_computation.30 | loop fusion | flops 4718592 | bytes 7340550 | tf_op jit(solution)/shard_map/convert_element_type | solution.py:88
  131.8 1.6 fusion.25
  133.5 32.8 %reduce-scatter.2.cloned.1.call-done = f32[128,288]{0,1:T(8,128)} async-done(((f32[128,2304]{0,1:T(8,128)}), f32[128,288]{0,1:T(8,128)}) %reduce-scatter.2.cloned.1.call-update) | async-done | bytes 147472 | tf_op jit(solution)/shard_map/reduce_scatter | solution.py:119
  166.3 43.3 %all-reduce.2.cloned.1.call-done = f32[128,288]{0,1:T(8,128)} async-done(((f32[128,288]{0,1:T(8,128)}), f32[128,288]{0,1:T(8,128)}) %all-reduce.2.cloned.1.call-update) | async-done | bytes 147472 | tf_op jit(solution)/shard_map/psum | solution.py:120
  209.7 3.3 %convolution_bitcast_fusion.1 = f32[128,32,64]{0,2,1:T(8,128)S(1)} fusion(f32[32,128]{1,0:T(8,128)S(1)} %bitcast.165, f32[32,128]{1,0:T(8,128)S(1)} %bitcast.159, f32[128,128]{0,1:T(8,128)S(1)} %copy-done.13, pred[128,128]{0,1:T(8,128)(4,1)S(1)} %copy-done.17, bf16[4,128,32,64]{1,3,2,0:T(8,128)(2,1)} %bitcast.145, s32[]{:T(128)S(6)} %select_n.83), kind=kOutput, calls=%fused_computation.17 | convolution fusion | flops 70254592 | bytes 1703940 | tf_op jit(solution)/shard_map/hts,shp->thp/dot_general | solution.py:89
  215.1 19.0 %all-gather.5.cloned.1.call-done = f32[128,2304]{0,1:T(8,128)} async-done(((f32[128,288]{0,1:T(8,128)}), f32[128,2304]{0,1:T(8,128)}) %all-gather.5.cloned.1.call-update) | async-done | bytes 1179664 | tf_op jit(solution)/shard_map/all_gather | solution.py:121
  234.1 1.3 broadcast_multiply_fusion
  235.5 1.4 copy.66
  (106 shorter events, 23.1 us)
Async XLA Ops:
  7.2 55.4 %copy-start = (bf16[128,2304]{1,0:T(8,128)(2,1)S(1)}, bf16[128,2304]{1,0:T(8,128)(2,1)}, u32[]{:S(2)}) copy-start(bf16[128,2304]{1,0:T(8,128)(2,1)} %param.11) | copy-start | bytes 1769476
  7.2 119.1 %all-gather.7.cloned.1.call-start = ((), (), s32[]{:S(2)}) async-start(), calls=%async_computation.4 | async-start | bytes 5242880 | tf_op jit(solution)/shard_map/all_gather | solution.py:79
  9.8 54.3 %copy-start.23 = (f32[128]{0:T(128)}, f32[128]{0:T(128)S(1)}, u32[]{:S(2)}) copy-start(f32[128]{0:T(128)S(1)} %add_multiply_fusion) | copy-start | bytes 1540
  64.2 13.2 %copy-start.1 = (bf16[512,2304]{1,0:T(8,128)(2,1)}, bf16[512,2304]{1,0:T(8,128)(2,1)S(1)}, u32[]{:S(2)}) copy-start(bf16[512,2304]{1,0:T(8,128)(2,1)S(1)} %convolution_convert_fusion) | copy-start | bytes 7077892
  67.4 11.6 %copy-start.7 = (f32[4,128,32]{2,1,0:T(8,128)}, f32[4,128,32]{2,1,0:T(8,128)S(1)}, u32[]{:S(2)}) copy-start(f32[4,128,32]{2,1,0:T(8,128)S(1)} %reduce_window_sum.35) | copy-start | bytes 196612
  77.1 89.1 %reduce-scatter.2.cloned.1.call-start = ((), (), s32[]{:S(2)}) async-start(), calls=%async_computation.1 | async-start | bytes 1327104 | tf_op jit(solution)/shard_map/reduce_scatter | solution.py:119
  79.6 12.3 %copy-start.6 = (bf16[1,128,2048]{1,2,0:T(8,128)(2,1)S(1)}, bf16[1,128,2048]{1,2,0:T(8,128)(2,1)}, u32[]{:S(2)}) copy-start(bf16[1,128,2048]{1,2,0:T(8,128)(2,1)} %copy.61) | copy-start | bytes 1572868
  82.8 11.5 %copy-start.2 = (bf16[4,128,2048]{1,2,0:T(8,128)(2,1)}, bf16[4,128,2048]{1,2,0:T(8,128)(2,1)S(1)}, u32[]{:S(2)}) copy-start(bf16[4,128,2048]{1,2,0:T(8,128)(2,1)S(1)} %copy.54) | copy-start | bytes 6291460
  89.5 6.7 %copy-start.14 = (f32[1,128,32]{1,0,2:T(1,128)}, f32[1,128,32]{1,0,2:T(1,128)S(1)}, u32[]{:S(2)}) copy-start(f32[1,128,32]{1,0,2:T(1,128)S(1)} %constant_dynamic-slice_fusion.2) | copy-start | bytes 49156
  89.5 6.7 %copy-start.16 = (pred[128,128]{0,1:T(8,128)(4,1)}, pred[128,128]{0,1:T(8,128)(4,1)S(1)}, u32[]{:S(2)}) copy-start(pred[128,128]{0,1:T(8,128)(4,1)S(1)} %iota_compare_fusion) | copy-start | bytes 49156
  90.4 5.8 %copy-start.12 = (f32[128,128]{0,1:T(8,128)}, f32[128,128]{0,1:T(8,128)S(1)}, u32[]{:S(2)}) copy-start(f32[128,128]{0,1:T(8,128)S(1)} %fusion.64) | copy-start | bytes 196612
  91.9 4.4 %copy-start.10 = (f32[1,128,32]{1,2,0:T(8,128)S(1)}, f32[1,128,32]{1,2,0:T(8,128)}, u32[]{:S(2)}) copy-start(f32[1,128,32]{1,2,0:T(8,128)} %copy.57) | copy-start | bytes 49156
  99.3 27.0 %copy-start.19 = (f32[32]{0:T(128)S(1)}, f32[32]{0:T(128)}, u32[]{:S(2)}) copy-start(f32[32]{0:T(128)} %get-tuple-element.14) | copy-start | bytes 388
  99.3 27.0 %copy-start.20 = (f32[32]{0:T(128)S(1)}, f32[32]{0:T(128)}, u32[]{:S(2)}) copy-start(f32[32]{0:T(128)} %get-tuple-element.15) | copy-start | bytes 388
  99.3 27.0 %copy-start.21 = (f32[32]{0:T(128)S(1)}, f32[32]{0:T(128)}, u32[]{:S(2)}) copy-start(f32[32]{0:T(128)} %get-tuple-element.16) | copy-start | bytes 388
  99.3 27.0 %copy-start.22 = (f32[32]{0:T(128)S(1)}, f32[32]{0:T(128)}, u32[]{:S(2)}) copy-start(f32[32]{0:T(128)} %get-tuple-element.17) | copy-start | bytes 388
  126.3 4.0 %copy-start.8 = (f32[128,32,64]{0,2,1:T(8,128)S(1)}, f32[128,32,64]{0,2,1:T(8,128)}, u32[]{:S(2)}) copy-start(f32[128,32,64]{0,2,1:T(8,128)} %convolution_bitcast_fusion) | copy-start | bytes 3145732
  126.3 4.0 %copy-start.9 = (f32[1,128,32]{1,2,0:T(8,128)S(1)}, f32[1,128,32]{1,2,0:T(8,128)}, u32[]{:S(2)}) copy-start(f32[1,128,32]{1,2,0:T(8,128)} %copy.64) | copy-start | bytes 49156
  131.4 78.3 %copy-start.11 = (f32[1,128,32]{1,2,0:T(8,128)S(1)}, f32[1,128,32]{1,2,0:T(8,128)}, u32[]{:S(2)}) copy-start(f32[1,128,32]{1,2,0:T(8,128)} %copy.57) | copy-start | bytes 49156
  131.4 78.3 %copy-start.13 = (f32[128,128]{0,1:T(8,128)S(1)}, f32[128,128]{0,1:T(8,128)}, u32[]{:S(2)}) copy-start(f32[128,128]{0,1:T(8,128)} %copy-done.12) | copy-start | bytes 196612
  131.4 78.3 %copy-start.15 = (f32[1,128,32]{1,0,2:T(1,128)S(1)}, f32[1,128,32]{1,0,2:T(1,128)}, u32[]{:S(2)}) copy-start(f32[1,128,32]{1,0,2:T(1,128)} %copy-done.14) | copy-start | bytes 49156
  131.4 78.3 %copy-start.17 = (pred[128,128]{0,1:T(8,128)(4,1)S(1)}, pred[128,128]{0,1:T(8,128)(4,1)}, u32[]{:S(2)}) copy-start(pred[128,128]{0,1:T(8,128)(4,1)} %copy-done.16) | copy-start | bytes 49156
  133.4 76.2 %all-reduce.2.cloned.1.call-start = ((), (), s32[]{:S(2)}) async-start(), calls=%async_computation.2 | async-start | bytes 294912 | tf_op jit(solution)/shard_map/psum | solution.py:120
  166.3 67.8 %all-gather.5.cloned.1.call-start = ((), (), s32[]{:S(2)}) async-start(), calls=%async_computation.3 | async-start | bytes 1327104 | tf_op jit(solution)/shard_map/all_gather | solution.py:121
  (9 other events, 17.6 us)
Sparse Core Ops, SparseCore 0:
  77.3 48.9 all-gather.6
  133.6 32.6 reduce-scatter.1
  169.2 40.4 all-reduce.1
  211.3 22.8 all-gather.4
where the time goes:
time: 245 us; the launch traced here: 243 us
  waiting for transfers between devices  119 us (49%)
  blocking collectives  44 us (18%)
  matrix products  27.7 us (11%)
  local copies, waits for them, and re-layouts  21.2 us (9%)
  between operations  16.2 us (7%)
  other arithmetic  15.3 us (6%)
    all_gather x1, blocking collectives, on_device(): all_codes = lax.all_gather(codes, ('tm', 'series'), axis=1, tiled=True)  44 us
    psum x1, waiting for transfers between devices, on_device(): share_grad = lax.psum(share_grad, 'tm')  43.3 us
    reduce_scatter x1, waiting for transfers between devices, on_device(): lax.psum_scatter(local_grad, 'series', scatter_dimension=1, tiled=True)  32.8 us
    all_gather x1, waiting for transfers between devices, on_device(): adjoint_all = lax.all_gather(adjoint_local, 'tm')  23.4 us
    all_gather x1, waiting for transfers between devices, on_device(): total_grad = lax.all_gather(share_grad, 'series', axis=1, tiled=True)  19 us
    unnamed x62, local copies, waits for them, and re-layouts  5.44 us
  transfers between devices with their start and end apart: 4, of which 4 were waited for; matrix products, arithmetic and copies ran while one was open for 13% of the time, Pallas kernels for 0%

commit v1 on v0

--- a/solution.py
+++ b/solution.py
@@ -5,6 +5,18 @@
 from jax.sharding import PartitionSpec as P
 
 code_ceiling = 2097152.0
+
+
+def doubled_up(x, axis, dim):
+    ways, here = (lax.axis_size(axis), lax.axis_index(axis))
+    grown, reach = (x, 1)
+    while reach < ways:
+        theirs = lax.ppermute(grown, axis, [(d, d ^ reach) for d in range(ways)])
+        mine_first = jnp.concatenate([grown, theirs], axis=dim)
+        theirs_first = jnp.concatenate([theirs, grown], axis=dim)
+        grown = jnp.where(here & reach == 0, mine_first, theirs_first)
+        reach = 2 * reach
+    return grown
 
 
 def decay_matrix(cum_decay):
@@ -27,7 +39,7 @@
     series_count = lax.axis_size("series")
     my_block = lax.axis_index("tm")
     my_series = lax.axis_index("series")
-    all_codes = lax.all_gather(codes, ("tm", "series"), axis=1, tiled=True)
+    all_codes = doubled_up(codes, ("tm", "series"), 1)
     row = lax.dynamic_index_in_dim(all_codes, owner_slot[my_series], axis=0, keepdims=False)
     reading = row.astype(fl)
     edge_float = edges.astype(fl)

time: 245 us -> 220 us (0.90)
  blocking collectives: 44 us -> 0 us
  starting transfers between devices: 0.34 us -> 10.5 us
  waiting for transfers between devices: 119 us -> 126 us
    all_gather x1 -> x0, blocking collectives: 44 us -> none  [on_device(): all_codes = lax.all_gather(codes, ('tm', 'series'), axis=1, tiled=True)]
    ppermute x0 -> x5, starting transfers between devices: none -> 10.1 us  [doubled_up(): theirs = lax.ppermute(grown, axis, [(d, d ^ reach) for d in range(ways)])]
    ppermute x0 -> x5, waiting for transfers between devices: none -> 4.41 us  [doubled_up(): theirs = lax.ppermute(grown, axis, [(d, d ^ reach) for d in range(ways)])]
    all_gather x1, waiting for transfers between devices: 23.4 us -> 26.6 us  [on_device(): adjoint_all = lax.all_gather(adjoint_local, 'tm')]
    unnamed x62 -> x61, local copies, waits for them, and re-layouts: 5.44 us -> 5.35 us
  transfers between devices with their start and end apart: 4 -> 9, of which waited for: 4 -> 8; matrix products, arithmetic and copies ran while one was open for 13% -> 17% of each run, Pallas kernels for 0% -> 0%
where the time goes in v1:
time: 220 us; the launch traced here: 219 us
  waiting for transfers between devices  126 us (57%)
  matrix products  27.8 us (13%)
  local copies, waits for them, and re-layouts  21.1 us (10%)
  other arithmetic  17 us (8%)
  between operations  16.2 us (7%)
  starting transfers between devices  10.5 us (5%)
    psum x1, waiting for transfers between devices, on_device(): share_grad = lax.psum(share_grad, 'tm')  43.2 us
    reduce_scatter x1, waiting for transfers between devices, on_device(): lax.psum_scatter(local_grad, 'series', scatter_dimension=1, tiled=True)  32.9 us
    all_gather x1, waiting for transfers between devices, on_device(): adjoint_all = lax.all_gather(adjoint_local, 'tm')  26.6 us
    all_gather x1, waiting for transfers between devices, on_device(): total_grad = lax.all_gather(share_grad, 'series', axis=1, tiled=True)  19 us
    ppermute x5, starting transfers between devices, doubled_up(): theirs = lax.ppermute(grown, axis, [(d, d ^ reach) for d in range(ways)])  10.1 us
    unnamed x61, local copies, waits for them, and re-layouts  5.35 us
    dynamic_slice x6, local copies, waits for them, and re-layouts, mine(): return lax.dynamic_index_in_dim(a, my_block, axis=0, keepdims=False)  4.94 us
    slice x2, local copies, waits for them, and re-layouts, on_device(): projected_all[:, :, :inner_width]  4.74 us
  transfers between devices with their start and end apart: 9, of which 8 were waited for; matrix products, arithmetic and copies ran while one was open for 17% of the time, Pallas kernels for 0%

profile of v1, /device:TPU:0, one launch (start us, length us, event | category | flops | bytes accessed | tf_op | source)
XLA Modules:
  0.0 218.7 jit_solution(3124431067188828443)
XLA Ops:
  9.6 2.9 %collective-permute-start.1 = (s32[8,32]{1,0:T(8,128)S(1)}, s32[8,32]{1,0:T(8,128)S(1)}, u32[]{:S(2)}, u32[]{:S(2)}) collective-permute-start(s32[8,32]{1,0:T(8,128)S(1)} %add_select_fusion.1), channel_id=1, source_target_pairs={{0,2},{1,3},{2,0},{3,1},{4,6},{5,7},{6,4},{7,5},{8,10},{9,11},{10,... | collective-permute-start | bytes 3080 | tf_op jit(solution)/shard_map/ppermute | solution.py:14
  12.5 1.6 collective-permute-done.1
  14.2 3.0 %collective-permute-start.2 = (s32[8,64]{1,0:T(8,128)S(1)}, s32[8,64]{1,0:T(8,128)S(1)}, u32[]{:S(2)}, u32[]{:S(2)}) collective-permute-start(s32[8,64]{1,0:T(8,128)S(1)} %add_select_fusion.2), channel_id=1, source_target_pairs={{0,4},{1,5},{2,6},{3,7},{4,0},{5,1},{6,2},{7,3},{8,12},{9,13},{10,... | collective-permute-start | bytes 6152 | tf_op jit(solution)/shard_map/ppermute | solution.py:14
  18.9 1.8 collective-permute-start.3
  22.5 1.8 collective-permute-start.4
  26.9 2.0 copy.57
  29.6 1.4 convert_reduce_fusion
  31.7 4.1 %fusion = f32[512,4]{0,1:T(4,128)S(1)} fusion(f32[4096]{0:T(1024)S(1)} %get-tuple-element.13, f32[4096]{0:T(1024)S(1)} %convert_element_type.97, f32[512]{0:T(512)S(1)} %bitcast.163, f32[4096,1]{0,1:T(1,128)S(1)} %bitcast.167, f32[4096,1]{0,1:T(1,128)S(1)} %bitcast.154, f32[4096,1]{0,1:T(1,128)S(1)} %bitcast.153, f32[4096,1]{0,1:T(1,128)S(1)} %sub.42), kind=kOutput, calls=%fused_computation.2 | convolution fusion | flops 107003904 | bytes 108544 | tf_op jit(solution)/shard_map/dot_general | solution.py:53
  36.0 1.6 convolution_convert_fusion
  42.3 1.5 copy.53
  46.5 2.0 fusion.59
  49.4 1.6 slice.98
  51.6 3.1 %copy.50 = bf16[4,128,2048]{1,2,0:T(8,128)(2,1)S(1)} copy(bf16[4,128,2048]{2,1,0:T(8,128)(2,1)} %slice.98) | data formatting | bytes 4194304 | tf_op jit(solution)/shard_map/slice | solution.py:60
  56.0 1.7 exponential_multiply_fusion
  64.0 2.4 %fusion.4 = bf16[128,128]{0,1:T(8,128)(2,1)S(1)} fusion(bf16[128,32,64]{0,2,1:T(8,128)(2,1)S(1)} %bitcast.149, f32[32,128]{1,0:T(8,128)S(1)} %bitcast.164, f32[32,128]{1,0:T(8,128)} %bitcast.156, pred[128,128]{0,1:T(8,128)(4,1)} %iota_compare_fusion, bf16[4,128,32,64]{1,3,2,0:T(8,128)(2,1)S(1)} %bitcast.143, s32[]{:T(128)S(6)} %select_n.133), kind=kOutput, calls=%fused_computation.9 | convolution fusion | flops 70238208 | bytes 1146884 | tf_op jit(solution)/shard_map/thp,shp->hts/dot_general | solution.py:114
  68.4 2.4 %convolution_bitcast_fusion = f32[128,32,64]{0,2,1:T(8,128)} fusion(bf16[128,32,64]{0,2,1:T(8,128)(2,1)S(1)} %bitcast.150, f32[32,128]{1,0:T(8,128)S(1)} %bitcast.165, f32[32,128]{1,0:T(8,128)S(1)} %bitcast.157, f32[128,128]{0,1:T(8,128)S(1)} %fusion.64, pred[128,128]{0,1:T(8,128)(4,1)S(1)} %copy-done.14), kind=kOutput, calls=%fused_computation.14 | convolution fusion | flops 70254592 | bytes 1687552 | tf_op jit(solution)/shard_map/hts,thp->shp/dot_general | solution.py:108
  71.5 3.6 %fusion.41 = f32[4,32,64,128]{3,2,1,0:T(8,128)} fusion(bf16[4,128,32,64]{1,3,2,0:T(8,128)(2,1)S(1)} %multiply_convert_fusion, bf16[4,128,2304]{2,1,0:T(8,128)(2,1)} %bitcast.142), kind=kOutput, calls=%fused_computation.67 | convolution fusion | flops 268435456 | bytes 6422528 | tf_op jit(solution)/shard_map/bthp,btn->bhpn/dot_general | solution.py:70
  75.1 26.6 %all-gather.6.cloned.1.call-done = f32[128,64,128]{2,1,0:T(8,128)} async-done(((f32[32,64,128]{2,1,0:T(8,128)}), f32[128,64,128]{2,1,0:T(8,128)}) %all-gather.6.cloned.1.call-update) | async-done | bytes 4194320 | tf_op jit(solution)/shard_map/all_gather | solution.py:91
  101.7 3.6 %fusion.15 = (bf16[1,32,64,128]{3,2,1,0:T(8,128)(2,1)S(1)}, bf16[1,32,64,128]{3,2,1,0:T(8,128)(2,1)S(1)}) fusion(f32[128,64,128]{2,1,0:T(8,128)} %all-gather.6.cloned.1.call-done, f32[32]{0:T(128)S(1)} %copy-done.19, f32[32]{0:T(128)S(1)} %copy-done.21, f32[32]{0:T(128)S(1)} %copy-done.22, pred[]{:T(512)S(6)} %lt.34, pred[]{:T(512)S(6)} %lt.33, pred[]{:T(512)S(6)} %lt.32, ...), kind=kLoop, calls=%fused_computation.30 | loop fusion | flops 4718592 | bytes 7340550 | tf_op jit(solution)/shard_map/convert_element_type | solution.py:100
  107.2 1.6 fusion.25
  108.9 32.9 %reduce-scatter.2.cloned.1.call-done = f32[128,288]{0,1:T(8,128)} async-done(((f32[128,2304]{0,1:T(8,128)}), f32[128,288]{0,1:T(8,128)}) %reduce-scatter.2.cloned.1.call-update) | async-done | bytes 147472 | tf_op jit(solution)/shard_map/reduce_scatter | solution.py:131
  141.8 43.2 %all-reduce.2.cloned.1.call-done = f32[128,288]{0,1:T(8,128)} async-done(((f32[128,288]{0,1:T(8,128)}), f32[128,288]{0,1:T(8,128)}) %all-reduce.2.cloned.1.call-update) | async-done | bytes 147472 | tf_op jit(solution)/shard_map/psum | solution.py:132
  185.1 3.3 %convolution_bitcast_fusion.1 = f32[128,32,64]{0,2,1:T(8,128)S(1)} fusion(f32[32,128]{1,0:T(8,128)S(1)} %bitcast.166, f32[32,128]{1,0:T(8,128)S(1)} %bitcast.158, f32[128,128]{0,1:T(8,128)S(1)} %copy-done.13, pred[128,128]{0,1:T(8,128)(4,1)S(1)} %copy-done.15, bf16[4,128,32,64]{1,3,2,0:T(8,128)(2,1)} %bitcast.144, s32[]{:T(128)S(6)} %select_n.133), kind=kOutput, calls=%fused_computation.17 | convolution fusion | flops 70254592 | bytes 1703940 | tf_op jit(solution)/shard_map/hts,shp->thp/dot_general | solution.py:101
  190.4 19.0 %all-gather.4.cloned.1.call-done = f32[128,2304]{0,1:T(8,128)} async-done(((f32[128,288]{0,1:T(8,128)}), f32[128,2304]{0,1:T(8,128)}) %all-gather.4.cloned.1.call-update) | async-done | bytes 1179664 | tf_op jit(solution)/shard_map/all_gather | solution.py:133
  (117 shorter events, 33.5 us)
Async XLA Ops:
  7.2 28.8 %copy-start = (bf16[128,2304]{1,0:T(8,128)(2,1)S(1)}, bf16[128,2304]{1,0:T(8,128)(2,1)}, u32[]{:S(2)}) copy-start(bf16[128,2304]{1,0:T(8,128)(2,1)} %param.11) | copy-start | bytes 1769476
  7.2 94.5 %all-gather.6.cloned.1.call-start = ((), (), s32[]{:S(2)}) async-start(), calls=%async_computation.4 | async-start | bytes 5242880 | tf_op jit(solution)/shard_map/all_gather | solution.py:91
  7.2 1.6 collective-permute-start
  9.6 4.5 %collective-permute-start.1 = (s32[8,32]{1,0:T(8,128)S(1)}, s32[8,32]{1,0:T(8,128)S(1)}, u32[]{:S(2)}, u32[]{:S(2)}) collective-permute-start(s32[8,32]{1,0:T(8,128)S(1)} %add_select_fusion.1), channel_id=1, source_target_pairs={{0,2},{1,3},{2,0},{3,1},{4,6},{5,7},{6,4},{7,5},{8,10},{9,11},{10,... | collective-permute-start | bytes 3080 | tf_op jit(solution)/shard_map/ppermute | solution.py:14
  14.2 4.6 %collective-permute-start.2 = (s32[8,64]{1,0:T(8,128)S(1)}, s32[8,64]{1,0:T(8,128)S(1)}, u32[]{:S(2)}, u32[]{:S(2)}) collective-permute-start(s32[8,64]{1,0:T(8,128)S(1)} %add_select_fusion.2), channel_id=1, source_target_pairs={{0,4},{1,5},{2,6},{3,7},{4,0},{5,1},{6,2},{7,3},{8,12},{9,13},{10,... | collective-permute-start | bytes 6152 | tf_op jit(solution)/shard_map/ppermute | solution.py:14
  18.9 3.6 %collective-permute-start.3 = (s32[8,128]{1,0:T(8,128)S(1)}, s32[8,128]{1,0:T(8,128)S(1)}, u32[]{:S(2)}, u32[]{:S(2)}) collective-permute-start(s32[8,128]{1,0:T(8,128)S(1)} %add_select_fusion.3), channel_id=1, source_target_pairs={{0,8},{1,9},{2,10},{3,11},{4,12},{5,13},{6,14},{7,15},{8,0},{9,1},... | collective-permute-start | bytes 12296 | tf_op jit(solution)/shard_map/ppermute | solution.py:14
  22.5 7.1 %collective-permute-start.4 = (s32[8,256]{1,0:T(8,128)S(1)}, s32[8,256]{1,0:T(8,128)S(1)}, u32[]{:S(2)}, u32[]{:S(2)}) collective-permute-start(s32[8,256]{1,0:T(8,128)S(1)} %add_select_fusion), channel_id=1, source_target_pairs={{0,16},{1,17},{2,18},{3,19},{4,20},{5,21},{6,22},{7,23},{8,24},{9,... | collective-permute-start | bytes 24584 | tf_op jit(solution)/shard_map/ppermute | solution.py:14
  24.4 13.2 %copy-start.23 = (f32[128]{0:T(128)}, f32[128]{0:T(128)S(1)}, u32[]{:S(2)}) copy-start(f32[128]{0:T(128)S(1)} %add_multiply_fusion) | copy-start | bytes 1540
  37.6 11.8 %copy-start.1 = (bf16[512,2304]{1,0:T(8,128)(2,1)}, bf16[512,2304]{1,0:T(8,128)(2,1)S(1)}, u32[]{:S(2)}) copy-start(bf16[512,2304]{1,0:T(8,128)(2,1)S(1)} %convolution_convert_fusion) | copy-start | bytes 7077892
  40.9 10.2 %copy-start.7 = (f32[4,128,32]{2,1,0:T(8,128)}, f32[4,128,32]{2,1,0:T(8,128)S(1)}, u32[]{:S(2)}) copy-start(f32[4,128,32]{2,1,0:T(8,128)S(1)} %reduce_window_sum.35) | copy-start | bytes 196612
  48.5 93.2 %reduce-scatter.2.cloned.1.call-start = ((), (), s32[]{:S(2)}) async-start(), calls=%async_computation.1 | async-start | bytes 1327104 | tf_op jit(solution)/shard_map/reduce_scatter | solution.py:131
  51.6 12.4 %copy-start.6 = (bf16[1,128,2048]{1,2,0:T(8,128)(2,1)S(1)}, bf16[1,128,2048]{1,2,0:T(8,128)(2,1)}, u32[]{:S(2)}) copy-start(bf16[1,128,2048]{1,2,0:T(8,128)(2,1)} %copy.57) | copy-start | bytes 1572868
  54.7 11.7 %copy-start.2 = (bf16[4,128,2048]{1,2,0:T(8,128)(2,1)}, bf16[4,128,2048]{1,2,0:T(8,128)(2,1)S(1)}, u32[]{:S(2)}) copy-start(bf16[4,128,2048]{1,2,0:T(8,128)(2,1)S(1)} %copy.50) | copy-start | bytes 6291460
  61.6 6.7 %copy-start.16 = (f32[1,128,32]{1,0,2:T(1,128)}, f32[1,128,32]{1,0,2:T(1,128)S(1)}, u32[]{:S(2)}) copy-start(f32[1,128,32]{1,0,2:T(1,128)S(1)} %constant_dynamic-slice_fusion.2) | copy-start | bytes 49156
  71.4 30.2 %copy-start.19 = (f32[32]{0:T(128)S(1)}, f32[32]{0:T(128)}, u32[]{:S(2)}) copy-start(f32[32]{0:T(128)} %get-tuple-element.14) | copy-start | bytes 388
  71.4 30.2 %copy-start.20 = (f32[32]{0:T(128)S(1)}, f32[32]{0:T(128)}, u32[]{:S(2)}) copy-start(f32[32]{0:T(128)} %get-tuple-element.15) | copy-start | bytes 388
  71.5 30.2 %copy-start.21 = (f32[32]{0:T(128)S(1)}, f32[32]{0:T(128)}, u32[]{:S(2)}) copy-start(f32[32]{0:T(128)} %get-tuple-element.16) | copy-start | bytes 388
  71.5 30.2 %copy-start.22 = (f32[32]{0:T(128)S(1)}, f32[32]{0:T(128)}, u32[]{:S(2)}) copy-start(f32[32]{0:T(128)} %get-tuple-element.17) | copy-start | bytes 388
  106.8 78.3 %copy-start.11 = (f32[1,128,32]{1,2,0:T(8,128)S(1)}, f32[1,128,32]{1,2,0:T(8,128)}, u32[]{:S(2)}) copy-start(f32[1,128,32]{1,2,0:T(8,128)} %copy.53) | copy-start | bytes 49156
  106.8 78.3 %copy-start.13 = (f32[128,128]{0,1:T(8,128)S(1)}, f32[128,128]{0,1:T(8,128)}, u32[]{:S(2)}) copy-start(f32[128,128]{0,1:T(8,128)} %copy-done.12) | copy-start | bytes 196612
  106.8 78.3 %copy-start.15 = (pred[128,128]{0,1:T(8,128)(4,1)S(1)}, pred[128,128]{0,1:T(8,128)(4,1)}, u32[]{:S(2)}) copy-start(pred[128,128]{0,1:T(8,128)(4,1)} %iota_compare_fusion) | copy-start | bytes 49156
  106.8 78.3 %copy-start.17 = (f32[1,128,32]{1,0,2:T(1,128)S(1)}, f32[1,128,32]{1,0,2:T(1,128)}, u32[]{:S(2)}) copy-start(f32[1,128,32]{1,0,2:T(1,128)} %copy-done.16) | copy-start | bytes 49156
  108.8 76.2 %all-reduce.2.cloned.1.call-start = ((), (), s32[]{:S(2)}) async-start(), calls=%async_computation.2 | async-start | bytes 294912 | tf_op jit(solution)/shard_map/psum | solution.py:132
  141.8 67.7 %all-gather.4.cloned.1.call-start = ((), (), s32[]{:S(2)}) async-start(), calls=%async_computation.3 | async-start | bytes 1327104 | tf_op jit(solution)/shard_map/all_gather | solution.py:133
  (14 other events, 40.2 us)
Sparse Core Ops, SparseCore 0:
  48.6 52.9 all-gather.5
  108.9 32.7 reduce-scatter.1
  144.7 40.2 all-reduce.1
  186.6 22.8 all-gather.3
